TPU v7x, 32 devices: a whole 2x2x4 slice. The times are simulated.
32 devices in a mesh: store: 4 (over x, core), blk: 2 (over y), batch: 4 (over z).
Axes of the slice: x: 2, y: 2, z: 4, core: 2. Of those that a mesh axis runs over, the one named last changes fastest.
Arguments:
- cands: bfloat16 [16, 256, 1024], P(('batch', 'store'), 'blk'), parts along dimension 0, may hold values from -6 to 6
- kv_store: bfloat16 [16, 512, 2, 1024], P('batch', ('blk', 'store')), parts along dimension 0, may hold values from -6 to 6
- proj_weight: bfloat16 [1024, 2, 1024], P(None, None, 'blk'), may hold values from -0.1875 to 0.1875
- norm_gain: float32 [1024], replicated, may hold values from 0.5 to 1.5
- users: int32 [16], P('batch'), parts along dimension 0, may hold values from 0 to 3, each once
- lengths: int32 [16], P('batch'), parts along dimension 0, may hold values from 128 to 512, as said below
Outputs:
- scored: bfloat16 [16, 256, 1024], P(('batch', 'store'), 'blk'), parts along dimension 0
There are 4 independent parts, one for each index of `batch`. A program takes and returns all parts, laid end to end along the dimension named above; an argument that names none is the same for every part. Nothing has to cross between parts.
Inputs may be any that keep to these rules, and one draw needn't show every extreme that they name: A permutation of the users. `lengths`: some user has all 512 events live.
All inputs are finite; a program needn't handle non-finite values.
Results may differ from a plain program's by a relative error of at most 0.014.
Values may be sent and summed in bfloat16 or wider, within the bound.
No kernel may reach another device: no remote copies, remote signals or barrier semaphores. Data moves between devices by JAX's collectives and lax.ppermute only.
A program may use at most 64 MiB of HBM per device.

v0:
```python
import jax
import jax.numpy as jnp
from jax import lax
from jax.sharding import PartitionSpec as P

D = 1024
HEADS = 8


def attend(query, keys, values, offset, count):
    head_size = D // HEADS
    inverse = head_size ** (-0.5)
    rows = query.shape[0]
    local_heads = query.shape[1] // head_size
    total = keys.shape[0]
    block = min(total, 256)
    qheads = query.reshape(rows, local_heads, head_size)
    scale_count = count.astype(jnp.float32)

    def one_block(index, accum):
        start = index * block
        key_block = lax.dynamic_slice_in_dim(keys, start, block, 0).reshape(
            block, local_heads, head_size
        )
        value_block = lax.dynamic_slice_in_dim(values, start, block, 0).reshape(
            block, local_heads, head_size
        )
        scores = (
            jnp.einsum("chd,khd->hck", qheads, key_block, preferred_element_type=jnp.float32)
            * inverse
        )
        live = (offset + start + jnp.arange(block) < count).astype(jnp.float32)
        weights = (jax.nn.silu(scores) * live[None, None, :] / scale_count).astype(jnp.bfloat16)
        part_sum = jnp.einsum(
            "hck,khd->chd", weights, value_block, preferred_element_type=jnp.float32
        )
        return accum + part_sum.reshape(rows, local_heads * head_size)

    empty = jnp.zeros((rows, local_heads * head_size), jnp.float32)
    return lax.fori_loop(0, total // block, one_block, empty)


def finish(attended, gate, norm_gain):
    wide = attended.astype(jnp.float32)
    mean = jnp.mean(wide, axis=1, keepdims=True)
    var = jnp.mean((wide - mean) ** 2, axis=1, keepdims=True)
    normed = (wide - mean) * lax.rsqrt(var + 1e-05) * norm_gain[None, :]
    return (normed * gate.astype(jnp.float32)).astype(jnp.bfloat16)


def per_device(cands, kv_store, proj_weight, norm_gain, users, lengths):
    slot = lax.axis_index("store")
    person = lax.dynamic_index_in_dim(users, slot, 0, keepdims=False)
    count = lax.dynamic_index_in_dim(lengths, person, 0, keepdims=False)
    ordered = jnp.take(kv_store, users, axis=0)
    feats = cands[0]
    fetched = lax.all_to_all(ordered, "store", split_axis=0, concat_axis=1, tiled=True)
    keys = fetched[0, :, 0, :]
    values = fetched[0, :, 1, :]
    offset = lax.axis_index("blk") * keys.shape[0]
    full_weight = lax.all_gather(proj_weight, "blk", axis=2, tiled=True)
    width = full_weight.shape[0]
    own_proj = jnp.dot(
        feats, full_weight.reshape(width, 2 * width), preferred_element_type=jnp.float32
    )
    own_query = own_proj[:, :width].astype(jnp.bfloat16)
    gate = jax.nn.silu(own_proj[:, width:]).astype(jnp.bfloat16)
    query = lax.all_gather(own_query, "blk", axis=0, tiled=True)
    attended = lax.psum_scatter(
        attend(query, keys, values, offset, count), "blk", scatter_dimension=0, tiled=True
    ).astype(jnp.bfloat16)
    return finish(attended, gate, norm_gain)[None]


def solution(mesh):
    in_specs = (
        P(("batch", "store"), "blk", None),
        P("batch", ("blk", "store"), None, None),
        P(None, None, "blk"),
        P(),
        P("batch"),
        P("batch"),
    )
    out_specs = P(("batch", "store"), "blk", None)
    return jax.shard_map(
        per_device, mesh=mesh, in_specs=in_specs, out_specs=out_specs, check_vma=False
    )
```

profile of v0, /device:TPU:0, one launch (start us, length us, event | category | flops | bytes accessed | tf_op | source)
XLA Modules:
  0.0 117.1 jit_solution(7535598614453149541)
XLA Ops:
  6.5 0.0 copy-start
  6.5 0.0 copy-start.3
  6.5 0.0 all-gather.2.cloned.1.call-start
  6.5 0.7 all-gather.2.cloned.1.call-update
  7.3 0.0 copy-done.3
  7.3 0.5 copy-done
  7.8 2.7 %gather_fusion = bf16[4,64,2,1024]{3,2,1,0:T(2,128)(2,1)S(1)} fusion(bf16[4,64,2,1024]{3,2,1,0:T(2,128)(2,1)S(1)} %copy-done, s32[1024]{0:T(1024)S(1)} %pad_clamp_fusion), kind=kCustom, calls=%fused_computation | custom fusion | bytes 2097168 | tf_op jit(solution)/shard_map/jit(_take)/gather | solution.py:55
  10.5 0.0 copy-start.4
  10.5 1.9 %broadcast_select_fusion = bf16[4,64,2,1024]{3,2,1,0:T(2,128)(2,1)} fusion(bf16[4,64,2,1024]{3,2,1,0:T(2,128)(2,1)S(1)} %gather_fusion, pred[4]{0:T(512)(128)(4,1)S(1)} %compare_and_fusion), kind=kLoop, calls=%fused_computation.2 | loop fusion | flops 524288 | bytes 2097156 | tf_op jit(solution)/shard_map/jit(_take)/select_n | solution.py:55
  12.4 4.2 %all-to-all-start = ((bf16[4,64,2,1024]{3,2,1,0:T(2,128)(2,1)}), bf16[4,64,2,1024]{3,2,1,0:T(2,128)(2,1)S(1)}, u32[]{:S(2)}, u32[]{:S(2)}) async-start(bf16[4,64,2,1024]{3,2,1,0:T(2,128)(2,1)} %broadcast_select_fusion), calls=%async_computation | async-start | bytes 2097152 | tf_op jit(solution)/shard_map/all_to_all | solution.py:57
  16.6 0.0 reduce-scatter.2.cloned.1.call-start
  16.6 0.6 dynamic_slice.11
  19.2 0.0 copy-done.4
  19.2 0.6 dynamic_slice.12
  20.4 0.7 compare_convert_fusion
  21.1 10.0 %all-to-all-done = bf16[4,64,2,1024]{3,2,1,0:T(2,128)(2,1)S(1)} async-done(((bf16[4,64,2,1024]{3,2,1,0:T(2,128)(2,1)}), bf16[4,64,2,1024]{3,2,1,0:T(2,128)(2,1)S(1)}, u32[]{:S(2)}, u32[]{:S(2)}) %all-to-all-start) | async-done | bytes 1048608 | tf_op jit(solution)/shard_map/all_to_all | solution.py:57
  31.1 0.3 copy.19
  31.4 0.1 fusion.20
  31.4 1.0 copy.20
  32.5 1.0 copy.21
  33.5 34.9 %all-gather.2.cloned.1.call-done = bf16[1024,2,1024]{2,1,0:T(2,128)(2,1)} async-done(((bf16[1024,2,512]{2,1,0:T(2,128)(2,1)}), bf16[1024,2,1024]{2,1,0:T(2,128)(2,1)}) %all-gather.2.cloned.1.call-update) | async-done | bytes 4194320 | tf_op jit(solution)/shard_map/all_gather | solution.py:61
  68.3 0.0 copy-start.1
  68.3 3.7 %copy.28 = bf16[128,8,2,1024]{3,1,2,0:T(8,128)(2,1)S(1)} copy(bf16[128,8,2,1024]{3,2,1,0:T(2,128)(2,1)} %bitcast.28) | data formatting | bytes 8388608
  72.0 0.0 copy-done.1
  72.0 0.7 fusion.15
  72.8 8.8 %all_gather.7 = bf16[256,1024]{1,0:T(8,128)(2,1)} all-gather(bf16[128,1024]{1,0:T(8,128)(2,1)S(1)} %slice.29), channel_id=1, replica_groups=mesh['store'=4,'blk'=2,'batch'=4] {'blk'}, dimensions={0}, use_global_device_ids=true | all-gather | bytes 786432 | tf_op jit(solution)/shard_map/all_gather | solution.py:68
  81.6 2.4 %fusion = f32[8,128,256]{2,1,0:T(8,128)S(1)} fusion(bf16[256,8,128]{0,2,1:T(8,128)(2,1)} %bitcast.31, bf16[256,8,128]{0,2,1:T(8,128)(2,1)} %bitcast.32, f32[]{:T(128)S(6)} %convert_element_type.32, f32[256]{0:T(256)S(1)} %compare_convert_fusion, bf16[256,1024]{1,0:T(8,128)(2,1)} %all_gather.7), kind=kOutput, calls=%fused_computation.3 | convolution fusion | flops 272629760 | bytes 2622468 | tf_op jit(solution)/shard_map/while/body/eval_jaxpr/hck,khd->chd/dot_general | solution.py:34
  84.1 0.0 copy-start.2
  84.1 1.3 %copy.26 = f32[256,1024]{1,0:T(8,128)} copy(f32[256,1024]{0,1:T(8,128)S(1)} %bitcast.30) | data formatting | bytes 2097152 | tf_op jit(solution)/shard_map/while/body/eval_jaxpr/reshape | solution.py:37
  85.4 0.0 reduce-scatter.2.cloned.1.call-update
  85.4 20.5 %reduce-scatter.2.cloned.1.call-done = f32[128,1024]{1,0:T(8,128)} async-done(((f32[256,1024]{1,0:T(8,128)}), f32[128,1024]{1,0:T(8,128)}) %reduce-scatter.2.cloned.1.call-update) | async-done | bytes 524304 | tf_op jit(solution)/shard_map/reduce_scatter | solution.py:69
  105.9 1.1 convert_reduce_fusion
  107.1 1.2 %fusion.7 = f32[128]{0:T(128)S(1)} fusion(f32[128]{0:T(128)S(1)} %broadcast_multiply_fusion, f32[128,1024]{1,0:T(8,128)} %reduce-scatter.2.cloned.1.call-done), kind=kLoop, calls=%fused_computation.12 | loop fusion | flops 655232 | bytes 525312 | tf_op jit(solution)/shard_map/reduce_sum | solution.py:46
  108.3 0.0 copy-done.2
  108.3 2.0 %fusion.17 = bf16[1,128,1024]{2,1,0:T(8,128)(2,1)} fusion(f32[128,2048]{1,0:T(8,128)S(1)} %fusion.15, f32[1024]{0:T(1024)S(1)} %copy-done.2, f32[128]{0:T(128)S(1)} %add_rsqrt_fusion, f32[128]{0:T(128)S(1)} %broadcast_multiply_fusion, f32[128,1024]{1,0:T(8,128)} %reduce-scatter.2.cloned.1.call-done), kind=kLoop, calls=%fused_computation.22 | loop fusion | flops 1703936 | bytes 1315840 | tf_op jit(solution)/shard_map/broadcast_in_dim | solution.py:72
  (6 shorter events, 0.1 us)
Async XLA Ops:
  6.5 1.2 %copy-start = (bf16[4,64,2,1024]{3,2,1,0:T(2,128)(2,1)S(1)}, bf16[4,64,2,1024]{3,2,1,0:T(2,128)(2,1)}, u32[]{:S(2)}) copy-start(bf16[4,64,2,1024]{3,2,1,0:T(2,128)(2,1)} %param.7) | copy-start | bytes 3145732
  6.5 0.7 copy-start.3
  6.5 61.8 %all-gather.2.cloned.1.call-start = ((), (), s32[]{:S(2)}) async-start(), calls=%async_computation.2 | async-start | bytes 6291456 | tf_op jit(solution)/shard_map/all_gather | solution.py:61
  10.5 8.7 %copy-start.4 = (s32[4]{0:T(128)S(1)}, s32[4]{0:T(128)}, u32[]{:S(2)}) copy-start(s32[4]{0:T(128)} %param.11) | copy-start | bytes 52
  12.4 18.7 %all-to-all-start = ((bf16[4,64,2,1024]{3,2,1,0:T(2,128)(2,1)}), bf16[4,64,2,1024]{3,2,1,0:T(2,128)(2,1)S(1)}, u32[]{:S(2)}, u32[]{:S(2)}) async-start(bf16[4,64,2,1024]{3,2,1,0:T(2,128)(2,1)} %broadcast_select_fusion), calls=%async_computation | async-start | bytes 2097152 | tf_op jit(solution)/shard_map/all_to_all | solution.py:57
  16.6 89.3 %reduce-scatter.2.cloned.1.call-start = ((), (), s32[]{:S(2)}) async-start(), calls=%async_computation.3 | async-start | bytes 1572864 | tf_op jit(solution)/shard_map/reduce_scatter | solution.py:69
  68.3 3.7 %copy-start.1 = (bf16[1,128,1024]{2,1,0:T(8,128)(2,1)S(1)}, bf16[1,128,1024]{2,1,0:T(8,128)(2,1)}, u32[]{:S(2)}) copy-start(bf16[1,128,1024]{2,1,0:T(8,128)(2,1)} %param.6) | copy-start | bytes 786436
  84.1 24.2 %copy-start.2 = (f32[1024]{0:T(1024)S(1)}, f32[1024]{0:T(1024)}, u32[]{:S(2)}) copy-start(f32[1024]{0:T(1024)} %param.9) | copy-start | bytes 12292
Sparse Core Ops, SparseCore 0:
  8.9 59.4 all-gather.1
  85.5 20.3 reduce-scatter.1
where the time goes:
time: 118 us; the launch traced here: 117 us
  waiting for transfers between devices  66.1 us (56%)
  between operations  16.1 us (14%)
  local copies, waits for them, and re-layouts  11.7 us (10%)
  blocking collectives  8.83 us (7%)
  other arithmetic  7 us (6%)
  starting transfers between devices  4.21 us (4%)
  matrix products  3.16 us (3%)
    all_gather x1, waiting for transfers between devices, per_device(): full_weight = lax.all_gather(proj_weight, 'blk', axis=2, tiled=True)  34.9 us
    reduce_scatter x1, waiting for transfers between devices, per_device(): lax.psum_scatter(attend(query, keys, values, offset, count), 'blk', scatt...  20.5 us
    all_to_all x1, waiting for transfers between devices, per_device(): lax.all_to_all(ordered, 'store', split_axis=0, concat_axis=1, tiled=True)  9.99 us
    all_gather x1, blocking collectives, per_device(): query = lax.all_gather(own_query, 'blk', axis=0, tiled=True)  8.83 us
    all_to_all x1, starting transfers between devices, per_device(): lax.all_to_all(ordered, 'store', split_axis=0, concat_axis=1, tiled=True)  4.21 us
    unnamed x11, local copies, waits for them, and re-layouts  4.18 us
    gather x1, local copies, waits for them, and re-layouts, per_device(): ordered = jnp.take(kv_store, users, axis=0)  2.65 us
    dot_general x1, matrix products, one_block(): jnp.einsum('hck,khd->chd', weights, value_block, preferred_element_type=j...  2.44 us
  transfers between devices with their start and end apart: 3, of which 3 were waited for; matrix products, arithmetic and copies ran while one was open for 8% of the time, Pallas kernels for 0%

commit v1 on v0

--- a/solution.py
+++ b/solution.py
@@ -58,7 +58,14 @@
     keys = fetched[0, :, 0, :]
     values = fetched[0, :, 1, :]
     offset = lax.axis_index("blk") * keys.shape[0]
-    full_weight = lax.all_gather(proj_weight, "blk", axis=2, tiled=True)
+    ways, here = (lax.axis_size("blk"), lax.axis_index("blk"))
+    full_weight, reach = (proj_weight, 1)
+    while reach < ways:
+        theirs = lax.ppermute(full_weight, "blk", [(d, d ^ reach) for d in range(ways)])
+        mine_first = jnp.concatenate([full_weight, theirs], axis=2)
+        theirs_first = jnp.concatenate([theirs, full_weight], axis=2)
+        full_weight = jnp.where(here & reach == 0, mine_first, theirs_first)
+        reach = 2 * reach
     width = full_weight.shape[0]
     own_proj = jnp.dot(
         feats, full_weight.reshape(width, 2 * width), preferred_element_type=jnp.float32

time: 118 us -> 111 us (0.941)
  waiting for transfers between devices: 66.1 us -> 52 us
  other arithmetic: 7 us -> 15.8 us
  local copies, waits for them, and re-layouts: 11.7 us -> 7.71 us
  starting transfers between devices: 4.21 us -> 6.52 us
  matrix products: 3.16 us -> 4.5 us
    all_gather x1 -> x0, waiting for transfers between devices: 34.9 us -> none  [per_device(): full_weight = lax.all_gather(proj_weight, 'blk', axis=2, tiled=True)]
    ppermute x0 -> x1, waiting for transfers between devices: none -> 20.5 us  [per_device(): lax.ppermute(full_weight, 'blk', [(d, d ^ reach) for d in range(ways)])]
    select_n x0 -> x1, other arithmetic: none -> 8.19 us  [per_device(): full_weight = jnp.where(here & reach == 0, mine_first, theirs_first)]
    ppermute x0 -> x1, starting transfers between devices: none -> 2.97 us  [per_device(): lax.ppermute(full_weight, 'blk', [(d, d ^ reach) for d in range(ways)])]
    unnamed x11, local copies, waits for them, and re-layouts: 4.18 us -> 1.45 us
    reshape x1 -> x0, local copies, waits for them, and re-layouts: 1.31 us -> none  [one_block(): return accum + part_sum.reshape(rows, local_heads * head_size)]
where the time goes in v1:
time: 111 us
  waiting for transfers between devices  52 us (47%)
  between operations  16.1 us (15%)
  other arithmetic  15.8 us (14%)
  blocking collectives  8.2 us (7%)
  local copies, waits for them, and re-layouts  7.71 us (7%)
  starting transfers between devices  6.52 us (6%)
  matrix products  4.5 us (4%)
    reduce_scatter x1, waiting for transfers between devices, per_device(): lax.psum_scatter(attend(query, keys, values, offset, count), 'blk', scatt...  21.6 us
    ppermute x1, waiting for transfers between devices, per_device(): lax.ppermute(full_weight, 'blk', [(d, d ^ reach) for d in range(ways)])  20.5 us
    all_to_all x1, waiting for transfers between devices, per_device(): lax.all_to_all(ordered, 'store', split_axis=0, concat_axis=1, tiled=True)  9.92 us
    all_gather x1, blocking collectives, per_device(): query = lax.all_gather(own_query, 'blk', axis=0, tiled=True)  8.2 us
    select_n x1, other arithmetic, per_device(): full_weight = jnp.where(here & reach == 0, mine_first, theirs_first)  8.19 us
    all_to_all x1, starting transfers between devices, per_device(): lax.all_to_all(ordered, 'store', split_axis=0, concat_axis=1, tiled=True)  3.51 us
    dot_general x1, matrix products, one_block(): jnp.einsum('hck,khd->chd', weights, value_block, preferred_element_type=j...  3.2 us
    ppermute x1, starting transfers between devices, per_device(): lax.ppermute(full_weight, 'blk', [(d, d ^ reach) for d in range(ways)])  2.97 us
  transfers between devices with their start and end apart: 3, of which 3 were waited for; matrix products, arithmetic and copies ran while one was open for 8% of the time, Pallas kernels for 0%

profile of v1, /device:TPU:0, one launch (start us, length us, event | category | flops | bytes accessed | tf_op | source)
XLA Modules:
  0.0 110.9 jit_solution(482676795490265480)
XLA Ops:
  6.5 0.0 copy-start
  6.5 0.0 copy-start.3
  6.5 0.0 copy-start.4
  6.5 3.0 %collective-permute-start = (bf16[1024,2,512]{2,1,0:T(2,128)(2,1)}, bf16[1024,2,512]{2,1,0:T(2,128)(2,1)}, u32[]{:S(2)}, u32[]{:S(2)}) collective-permute-start(bf16[1024,2,512]{2,1,0:T(2,128)(2,1)} %param.8), channel_id=1, source_target_pairs={{0,4},{4,0},{1,5},{5,1},{2,6},{6,2},{3,7},{7,3},{8,12},{12,8},{9,1... | collective-permute-start | bytes 6291464 | tf_op jit(solution)/shard_map/ppermute | solution.py:64
  9.5 0.7 compare_select_fusion
  10.2 0.0 copy-done
  10.2 2.7 %gather_fusion = bf16[4,64,2,1024]{3,2,1,0:T(2,128)(2,1)S(1)} fusion(bf16[4,64,2,1024]{3,2,1,0:T(2,128)(2,1)S(1)} %copy-done, s32[1024]{0:T(1024)S(1)} %pad_clamp_fusion), kind=kCustom, calls=%fused_computation | custom fusion | bytes 2097168 | tf_op jit(solution)/shard_map/jit(_take)/gather | solution.py:55
  12.8 0.7 compare_and_fusion
  13.5 2.0 %broadcast_select_fusion.1 = bf16[4,64,2,1024]{3,2,1,0:T(2,128)(2,1)} fusion(bf16[4,64,2,1024]{3,2,1,0:T(2,128)(2,1)S(1)} %gather_fusion, pred[4]{0:T(512)(128)(4,1)S(1)} %compare_and_fusion), kind=kLoop, calls=%fused_computation.4 | loop fusion | flops 524288 | bytes 2097156 | tf_op jit(solution)/shard_map/jit(_take)/select_n | solution.py:55
  15.5 3.5 %all-to-all-start = ((bf16[4,64,2,1024]{3,2,1,0:T(2,128)(2,1)}), bf16[4,64,2,1024]{3,2,1,0:T(2,128)(2,1)S(1)}, u32[]{:S(2)}, u32[]{:S(2)}) async-start(bf16[4,64,2,1024]{3,2,1,0:T(2,128)(2,1)} %broadcast_select_fusion.1), calls=%async_computation | async-start | bytes 2097152 | tf_op jit(solution)/shard_map/all_to_all | solution.py:57
  19.0 0.0 reduce-scatter.2.cloned.1.call-start
  19.1 0.0 copy-done.3
  19.1 0.6 dynamic_slice.11
  21.6 0.0 copy-done.4
  21.6 0.6 dynamic_slice.12
  22.9 0.7 compare_convert_fusion
  23.5 9.9 %all-to-all-done = bf16[4,64,2,1024]{3,2,1,0:T(2,128)(2,1)S(1)} async-done(((bf16[4,64,2,1024]{3,2,1,0:T(2,128)(2,1)}), bf16[4,64,2,1024]{3,2,1,0:T(2,128)(2,1)S(1)}, u32[]{:S(2)}, u32[]{:S(2)}) %all-to-all-start) | async-done | bytes 1048608 | tf_op jit(solution)/shard_map/all_to_all | solution.py:57
  33.4 0.3 copy.19
  33.7 0.1 fusion.15
  33.8 0.2 copy.20
  34.0 1.0 copy.21
  35.0 20.5 %collective-permute-done = bf16[1024,2,512]{2,1,0:T(2,128)(2,1)} collective-permute-done((bf16[1024,2,512]{2,1,0:T(2,128)(2,1)}, bf16[1024,2,512]{2,1,0:T(2,128)(2,1)}, u32[]{:S(2)}, u32[]{:S(2)}) %collective-permute-start) | collective-permute-done | bytes 2097184 | tf_op jit(solution)/shard_map/ppermute | solution.py:64
  55.5 8.2 %broadcast_select_fusion = bf16[1024,2,1024]{2,1,0:T(2,128)(2,1)S(1)} fusion(pred[]{:T(512)S(6)} %eq.3, bf16[1024,2,512]{2,1,0:T(2,128)(2,1)} %collective-permute-done, bf16[1024,2,512]{2,1,0:T(2,128)(2,1)} %param.8), kind=kLoop, calls=%fused_computation.1 | loop fusion | flops 18874368 | bytes 8388609 | tf_op jit(solution)/shard_map/jit(_where)/select_n | solution.py:67
  63.6 0.0 copy-start.1
  63.7 1.4 %copy.27 = bf16[128,8,2,1024]{3,1,2,0:T(8,128)(2,1)S(1)} copy(bf16[128,8,2,1024]{3,2,1,0:T(2,128)(2,1)S(1)} %bitcast.23) | data formatting | bytes 8388608
  65.1 0.0 copy-done.1
  65.1 1.3 %convolution_bitcast_fusion = f32[128,2048]{0,1:T(8,128)S(1)} fusion(bf16[1024,2048]{1,0:T(8,128)(2,1)S(1)} %bitcast.22, bf16[1,128,1024]{2,1,0:T(8,128)(2,1)S(1)} %copy-done.1), kind=kOutput, calls=%fused_computation.2 | convolution fusion | flops 536870912 | bytes 5505024 | tf_op jit(solution)/shard_map/dot_general | solution.py:70
  66.5 8.2 %all_gather.3 = bf16[256,1024]{0,1:T(8,128)(2,1)S(1)} all-gather(bf16[128,1024]{0,1:T(8,128)(2,1)S(1)} %slice.29), channel_id=1, replica_groups=mesh['store'=4,'blk'=2,'batch'=4] {'blk'}, dimensions={0}, use_global_device_ids=true | all-gather | bytes 786432 | tf_op jit(solution)/shard_map/all_gather | solution.py:75
  74.7 0.0 copy-start.2
  74.7 3.2 %fusion = f32[8,128,256]{2,1,0:T(8,128)} fusion(bf16[256,8,128]{0,2,1:T(8,128)(2,1)S(1)} %bitcast.27, bf16[256,8,128]{0,2,1:T(8,128)(2,1)S(1)} %bitcast.26, bf16[256,8,128]{0,2,1:T(8,128)(2,1)} %bitcast.28, f32[]{:T(128)S(6)} %convert_element_type.32, f32[256]{0:T(256)S(1)} %compare_convert_fusion), kind=kOutput, calls=%fused_computation.5 | convolution fusion | flops 272629760 | bytes 2622468 | tf_op jit(solution)/shard_map/while/body/eval_jaxpr/hck,khd->chd/dot_general | solution.py:34
  77.9 0.0 reduce-scatter.2.cloned.1.call-update
  77.9 21.6 %reduce-scatter.2.cloned.1.call-done = f32[128,1024]{0,1:T(8,128)} async-done(((f32[256,1024]{0,1:T(8,128)}), f32[128,1024]{0,1:T(8,128)}) %reduce-scatter.2.cloned.1.call-update) | async-done | bytes 524304 | tf_op jit(solution)/shard_map/reduce_scatter | solution.py:76
  99.5 1.2 %convert_reduce_fusion = f32[128]{0:T(128)S(1)} fusion(f32[128,1024]{0,1:T(8,128)} %reduce-scatter.2.cloned.1.call-done), kind=kLoop, calls=%fused_computation.11 | loop fusion | flops 393088 | bytes 524800 | tf_op jit(solution)/shard_map/reduce_sum | solution.py:45
  100.7 1.2 %fusion.7 = f32[128]{0:T(128)S(1)} fusion(f32[128]{0:T(128)S(1)} %broadcast_multiply_fusion, f32[128,1024]{0,1:T(8,128)} %reduce-scatter.2.cloned.1.call-done), kind=kLoop, calls=%fused_computation.14 | loop fusion | flops 655232 | bytes 525312 | tf_op jit(solution)/shard_map/reduce_sum | solution.py:46
  101.9 0.0 copy-done.2
  101.9 1.3 %fusion.12 = bf16[1,128,1024]{1,2,0:T(8,128)(2,1)S(1)} fusion(f32[128,2048]{0,1:T(8,128)S(1)} %convolution_bitcast_fusion, f32[1024]{0:T(1024)S(1)} %copy-done.2, f32[128]{0:T(128)S(1)} %add_rsqrt_fusion, f32[128]{0:T(128)S(1)} %broadcast_multiply_fusion, f32[128,1024]{0,1:T(8,128)} %reduce-scatter.2.cloned.1.call-done), kind=kLoop, calls=%fused_computation.21 | loop fusion | flops 1703936 | bytes 1315840 | tf_op jit(solution)/shard_map/broadcast_in_dim | solution.py:79
  103.2 0.9 copy.24
  (4 shorter events, 0.1 us)
Async XLA Ops:
  6.5 3.6 %copy-start = (bf16[4,64,2,1024]{3,2,1,0:T(2,128)(2,1)S(1)}, bf16[4,64,2,1024]{3,2,1,0:T(2,128)(2,1)}, u32[]{:S(2)}) copy-start(bf16[4,64,2,1024]{3,2,1,0:T(2,128)(2,1)} %param.7) | copy-start | bytes 3145732
  6.5 12.5 %copy-start.3 = (s32[4]{0:T(128)S(1)}, s32[4]{0:T(128)}, u32[]{:S(2)}) copy-start(s32[4]{0:T(128)} %param.10) | copy-start | bytes 52
  6.5 15.1 %copy-start.4 = (s32[4]{0:T(128)S(1)}, s32[4]{0:T(128)}, u32[]{:S(2)}) copy-start(s32[4]{0:T(128)} %param.11) | copy-start | bytes 52
  6.5 48.9 %collective-permute-start = (bf16[1024,2,512]{2,1,0:T(2,128)(2,1)}, bf16[1024,2,512]{2,1,0:T(2,128)(2,1)}, u32[]{:S(2)}, u32[]{:S(2)}) collective-permute-start(bf16[1024,2,512]{2,1,0:T(2,128)(2,1)} %param.8), channel_id=1, source_target_pairs={{0,4},{4,0},{1,5},{5,1},{2,6},{6,2},{3,7},{7,3},{8,12},{12,8},{9,1... | collective-permute-start | bytes 6291464 | tf_op jit(solution)/shard_map/ppermute | solution.py:64
  15.5 18.0 %all-to-all-start = ((bf16[4,64,2,1024]{3,2,1,0:T(2,128)(2,1)}), bf16[4,64,2,1024]{3,2,1,0:T(2,128)(2,1)S(1)}, u32[]{:S(2)}, u32[]{:S(2)}) async-start(bf16[4,64,2,1024]{3,2,1,0:T(2,128)(2,1)} %broadcast_select_fusion.1), calls=%async_computation | async-start | bytes 2097152 | tf_op jit(solution)/shard_map/all_to_all | solution.py:57
  19.0 80.5 %reduce-scatter.2.cloned.1.call-start = ((), (), s32[]{:S(2)}) async-start(), calls=%async_computation.2 | async-start | bytes 1572864 | tf_op jit(solution)/shard_map/reduce_scatter | solution.py:76
  63.6 1.5 %copy-start.1 = (bf16[1,128,1024]{2,1,0:T(8,128)(2,1)S(1)}, bf16[1,128,1024]{2,1,0:T(8,128)(2,1)}, u32[]{:S(2)}) copy-start(bf16[1,128,1024]{2,1,0:T(8,128)(2,1)} %param.6) | copy-start | bytes 786436
  74.7 27.2 %copy-start.2 = (f32[1024]{0:T(1024)S(1)}, f32[1024]{0:T(1024)}, u32[]{:S(2)}) copy-start(f32[1024]{0:T(1024)} %param.9) | copy-start | bytes 12292
Sparse Core Ops, SparseCore 0:
  78.0 21.4 reduce-scatter.1
